TPU v7x, 256 devices: a whole 4x4x8 slice. The times are simulated.
256 devices in a mesh: attn: 32 (over z, y), expert: 4 (over x), rep: 2 (over core).
Axes of the slice: x: 4, y: 4, z: 8, core: 2. Of those that a mesh axis runs over, the one named last changes fastest.
Arguments:
- queries: bfloat16 [256, 73728], P('attn', ('expert', 'rep')), may hold values from -120 to 120
- new_latent: bfloat16 [256, 576], P('attn'), may hold values from -6 to 6
- cache_pool: bfloat16 [16384, 576], P('attn'), may hold values from -6 to 6
- local_len: int32 [32, 4], P('attn'), may hold values from 1 to 384, 512 in all within a row
- spill_cache: bfloat16 [1024, 16, 576], P('attn'), may hold values from -6 to 6
- spill_owner: int32 [1024], replicated, may hold values from -1 to 127, as said below
- w_uv: bfloat16 [128, 512, 128], P(('expert', 'rep')), may hold values from -0.25 to 0.25
- w_o: bfloat16 [16384, 7168], P(('expert', 'rep'), 'attn'), may hold values from -0.046875 to 0.046875
- residual: bfloat16 [256, 7168], P(None, 'attn'), may hold values from -3 to 3
- norm_gain: float32 [7168], replicated, may hold values from 0.5 to 1.5
- route_ids: int32 [256, 4], replicated, may hold values from 0 to 15, all different within a row; in each aligned block of 128 rows (0 to 127, 128 to 255, ...) at most 40 rows name the same one
- route_scores: float32 [256, 4], replicated, may hold values from 0.05 to 1
- w_gate: bfloat16 [7168, 32768], P(None, ('attn', 'expert')), may hold values from -0.0625 to 0.0625
- w_up: bfloat16 [7168, 32768], P(None, ('attn', 'expert')), may hold values from -0.0625 to 0.0625
- w_down: bfloat16 [32768, 7168], P(('attn', 'expert')), may hold values from -0.125 to 0.125
Outputs:
- mixed: bfloat16 [256, 7168], P('rep', ('attn', 'expert'))
Inputs may be any that keep to these rules, and one draw needn't show every extreme that they name: Each row of local_len sums to 512. `spill_owner`: each entry is -1 or the number of a request that lives on another index of attn than the block's slot. The slots of one index of attn hold at most 2 blocks of the requests of any one other index, and some index holds exactly 2 for some other index in every draw. `route_ids`: the token rows fall into 2 aligned blocks of 128 rows in order (2 being the size of rep); in each block no expert is named by more than 40 rows, and in some block one is named by exactly 40.
All inputs are finite; a program needn't handle non-finite values.
Results may differ from a plain program's by a relative error of at most 0.025.
Values may be sent and summed in bfloat16 or wider, within the bound.
No kernel may reach another device: no remote copies, remote signals or barrier semaphores. Data moves between devices by JAX's collectives and lax.ppermute only.
A program may use at most 128 MiB of HBM per device.

v0:
```python
import jax
import jax.numpy as jnp
from jax import lax
from jax.sharding import PartitionSpec as P

ROPE = 64
VH = 128
EXPERTS = 16
TOP = 4
MAXLOC = 384
CAP = 2
floor_score = -1e30
scale_out = 2.5


def expert_tables(route_ids, part_index, part_count, capacity):
    row_count = route_ids.shape[0] // part_count
    route_part = lax.dynamic_slice_in_dim(route_ids, part_index * row_count, row_count, 0)
    member = jnp.any(
        route_part[:, :, None] == jnp.arange(EXPERTS, dtype=jnp.int32)[None, None, :], axis=1
    )
    order_rank = jnp.cumsum(member.astype(jnp.int32), axis=0) - 1
    slot_ids = jnp.arange(capacity, dtype=jnp.int32)
    slot_hit = member[None, :, :] & (order_rank[None, :, :] == slot_ids[:, None, None])
    place_ids = jnp.arange(row_count, dtype=jnp.int32)
    slot_token = jnp.sum(jnp.where(slot_hit, place_ids[None, :, None], 0), axis=1)
    filled = jnp.any(slot_hit, axis=1)
    return (slot_token.T, filled.T, route_part)


def per_device(
    queries,
    new_latent,
    cache_pool,
    local_len,
    spill_cache,
    spill_owner,
    w_uv,
    w_o,
    residual,
    norm_gain,
    route_ids,
    route_scores,
    w_gate,
    w_up,
    w_down,
):
    n_attn = lax.axis_size("attn")
    n_expert = lax.axis_size("expert")
    n_rep = lax.axis_size("rep")
    attn_here = lax.axis_index("attn")
    expert_here = lax.axis_index("expert")
    rep_here = lax.axis_index("rep")
    req_count = local_len.shape[1]
    head_count = w_uv.shape[0]
    row_width = new_latent.shape[1]
    lat_width = w_uv.shape[1]
    score_scale = float(VH + ROPE) ** (-0.5)
    query_rows = queries.reshape(req_count, 2, head_count, row_width)
    lengths = local_len[0]
    starts = jnp.cumsum(lengths) - lengths
    padded = jnp.concatenate([cache_pool, jnp.zeros((MAXLOC, row_width), cache_pool.dtype)], axis=0)
    windows = jax.vmap(lambda start_one: lax.dynamic_slice_in_dim(padded, start_one, MAXLOC, 0))(
        starts
    )
    local_scores = (
        jnp.einsum("rthc,rkc->rthk", query_rows, windows, preferred_element_type=jnp.float32)
        * score_scale
    )
    inside = jnp.arange(MAXLOC)[None, :] < lengths[:, None]
    local_scores = jnp.where(inside[:, None, None, :], local_scores, floor_score)
    fresh_keys = new_latent.reshape(req_count, 2, row_width)
    fresh_scores = (
        jnp.einsum("rthc,rkc->rthk", query_rows, fresh_keys, preferred_element_type=jnp.float32)
        * score_scale
    )
    causal = jnp.arange(2)[None, :] <= jnp.arange(2)[:, None]
    fresh_scores = jnp.where(causal[None, :, None, :], fresh_scores, floor_score)
    spill_count = spill_cache.shape[0]
    directory = spill_owner.reshape(n_attn, spill_count)
    owner_dev = jnp.where(directory >= 0, directory // req_count, -1)
    earlier = jnp.arange(spill_count)[:, None] > jnp.arange(spill_count)[None, :]
    same_owner = owner_dev[:, :, None] == owner_dev[:, None, :]
    order_rank = jnp.sum(same_owner & earlier[None, :, :], axis=2)
    slot_ids = jnp.arange(CAP)
    own_row = owner_dev[attn_here]
    own_rank = order_rank[attn_here]
    pick_slot = (own_row[None, None, :] == jnp.arange(n_attn)[:, None, None]) & (
        own_rank[None, None, :] == slot_ids[None, :, None]
    )
    outgoing = jnp.einsum(
        "dks,sbc->dkbc",
        pick_slot.astype(jnp.bfloat16),
        spill_cache,
        preferred_element_type=jnp.float32,
    ).astype(jnp.bfloat16)
    incoming = lax.all_to_all(outgoing, "attn", split_axis=0, concat_axis=0, tiled=True)
    mine_slot = (owner_dev[:, None, :] == attn_here) & (
        order_rank[:, None, :] == slot_ids[None, :, None]
    )
    present = jnp.any(mine_slot, axis=2).reshape(-1)
    request = jnp.sum(
        jnp.where(mine_slot, directory[:, None, :] - attn_here * req_count, 0), axis=2
    ).reshape(-1)
    blocks = incoming.reshape(n_attn * CAP, incoming.shape[2], row_width)
    slot_query = jnp.take(query_rows, request, axis=0)
    spill_scores = (
        jnp.einsum("nthc,nbc->nthb", slot_query, blocks, preferred_element_type=jnp.float32)
        * score_scale
    )
    spill_scores = jnp.where(present[:, None, None, None], spill_scores, floor_score)
    belong = (request[None, :] == jnp.arange(req_count)[:, None]) & present[None, :]
    spill_top = jnp.max(
        jnp.where(belong[:, :, None, None], jnp.max(spill_scores, axis=3)[None], floor_score),
        axis=1,
    )
    row_top = jnp.maximum(
        jnp.maximum(jnp.max(local_scores, axis=3), jnp.max(fresh_scores, axis=3)), spill_top
    )
    local_weight = jnp.exp(local_scores - row_top[..., None])
    fresh_weight = jnp.exp(fresh_scores - row_top[..., None])
    spill_weight = jnp.exp(spill_scores - jnp.take(row_top, request, axis=0)[..., None])
    spill_weight = jnp.where(present[:, None, None, None], spill_weight, 0.0)
    belong_f = belong.astype(jnp.float32)
    denominator = jnp.sum(local_weight, axis=3) + jnp.sum(fresh_weight, axis=3)
    denominator = denominator + jnp.einsum(
        "rn,nth->rth", belong_f, jnp.sum(spill_weight, axis=3), precision=lax.Precision.HIGHEST
    )
    numerator = jnp.einsum(
        "rthk,rkc->rthc",
        local_weight.astype(jnp.bfloat16),
        windows[:, :, :lat_width],
        preferred_element_type=jnp.float32,
    )
    numerator = numerator + jnp.einsum(
        "rthk,rkc->rthc",
        fresh_weight.astype(jnp.bfloat16),
        fresh_keys[:, :, :lat_width],
        preferred_element_type=jnp.float32,
    )
    spill_numer = jnp.einsum(
        "nthb,nbc->nthc",
        spill_weight.astype(jnp.bfloat16),
        blocks[:, :, :lat_width],
        preferred_element_type=jnp.float32,
    )
    numerator = numerator + jnp.einsum(
        "rn,nthc->rthc", belong_f, spill_numer, precision=lax.Precision.HIGHEST
    )
    attended = (numerator / denominator[..., None]).astype(jnp.bfloat16)
    values = jnp.einsum(
        "rthc,hcv->rthv", attended, w_uv, preferred_element_type=jnp.float32
    ).astype(jnp.bfloat16)
    values = values.reshape(2 * req_count, head_count * w_uv.shape[2])
    partial_cols = jnp.dot(
        lax.all_gather(values, "attn", axis=0, tiled=True), w_o, preferred_element_type=jnp.float32
    )
    attn_cols = lax.psum(partial_cols.astype(jnp.bfloat16), ("expert", "rep")).astype(jnp.float32)
    hidden_cols = (residual.astype(jnp.float32) + attn_cols).astype(jnp.bfloat16)
    rows_part = route_ids.shape[0] // n_rep
    capacity = rows_part * TOP // EXPERTS * 5 // 4
    shards = n_attn * n_expert // EXPERTS
    slot_token, filled, route_part = expert_tables(route_ids, rep_here, n_rep, capacity)
    part_cols = lax.dynamic_slice_in_dim(hidden_cols, rep_here * rows_part, rows_part, 0)
    dest_expert = (jnp.arange(n_attn) * n_expert + expert_here) // shards
    send_rows = jnp.take(slot_token, dest_expert, axis=0)
    send_ok = jnp.take(filled, dest_expert, axis=0)
    outgoing_rows = jnp.where(
        send_ok[:, :, None], jnp.take(part_cols, send_rows, axis=0), jnp.zeros((), jnp.bfloat16)
    )
    outgoing_rows = outgoing_rows[:, :, None, :]
    received = lax.all_to_all(outgoing_rows, "attn", split_axis=0, concat_axis=2, tiled=True)
    item_count = received.shape[1]
    full_rows = received.reshape(item_count, -1)
    widened = full_rows.astype(jnp.float32)
    normed = (
        widened * lax.rsqrt(jnp.mean(widened * widened, axis=1, keepdims=True) + 1e-06) * norm_gain
    ).astype(jnp.bfloat16)
    gate_proj = jnp.dot(normed, w_gate, preferred_element_type=jnp.float32)
    up_proj = jnp.dot(normed, w_up, preferred_element_type=jnp.float32)
    activated = (jax.nn.silu(gate_proj) * up_proj).astype(jnp.bfloat16)
    result = jnp.dot(activated, w_down, preferred_element_type=jnp.float32)
    returned_block = lax.all_to_all(
        result.reshape(1, item_count, n_attn * n_expert, -1).astype(jnp.bfloat16),
        ("attn", "expert"),
        split_axis=2,
        concat_axis=0,
        tiled=True,
    ).astype(jnp.float32)
    returned = returned_block.reshape(n_attn * n_expert, item_count, -1)
    share_part = lax.dynamic_slice_in_dim(route_scores, rep_here * rows_part, rows_part, 0)
    share_part = share_part / jnp.sum(share_part, axis=1, keepdims=True)
    share_table = jnp.sum(
        jnp.where(
            route_part[:, :, None] == jnp.arange(EXPERTS, dtype=jnp.int32)[None, None, :],
            share_part[:, :, None],
            0.0,
        ),
        axis=1,
    )
    source_expert = jnp.arange(n_attn * n_expert) // shards
    back_rows = jnp.take(slot_token, source_expert, axis=0)
    back_ok = jnp.take(filled, source_expert, axis=0)
    weight_coef = (
        jnp.where(back_ok, share_table[back_rows, source_expert[:, None]], 0.0) * scale_out
    )
    sub_cols = returned.shape[2]
    weighted = (weight_coef[:, :, None] * returned).reshape(-1, sub_cols)
    routed = jax.ops.segment_sum(weighted, back_rows.reshape(-1), num_segments=rows_part)
    own_cols = lax.dynamic_slice_in_dim(part_cols, expert_here * sub_cols, sub_cols, 1)
    return (own_cols.astype(jnp.float32) + routed).astype(jnp.bfloat16)


def solution(mesh):
    return jax.shard_map(
        per_device,
        mesh=mesh,
        in_specs=(
            P("attn", ("expert", "rep")),
            P("attn", None),
            P("attn", None),
            P("attn", None),
            P("attn", None, None),
            P(),
            P(("expert", "rep"), None, None),
            P(("expert", "rep"), "attn"),
            P(None, "attn"),
            P(),
            P(),
            P(),
            P(None, ("attn", "expert")),
            P(None, ("attn", "expert")),
            P(("attn", "expert"), None),
        ),
        out_specs=P("rep", ("attn", "expert")),
        check_vma=False,
    )
```

profile of v0, /device:TPU:1, one launch (start us, length us, event | category | flops | bytes accessed | tf_op | source)
XLA Modules:
  0.0 364.1 jit_solution(18145144369421537697)
XLA Ops:
  6.5 0.9 reshape.649
  7.5 0.8 convert_reduce_fusion
  8.3 1.6 convolution_convert_fusion.1
  9.9 1.5 copy.175
  11.4 12.3 %all-to-all-start = ((bf16[32,2,16,576]{3,2,1,0:T(8,128)(2,1)}), bf16[32,2,16,576]{3,2,1,0:T(8,128)(2,1)}, u32[]{:S(2)}, u32[]{:S(2)}) async-start(bf16[32,2,16,576]{3,2,1,0:T(8,128)(2,1)} %copy.175), calls=%async_computation | async-start | bytes 2621440 | tf_op jit(solution)/shard_map/all_to_all | solution.py:97
  25.2 1.1 copy.169
  26.3 2.4 gather_fusion
  28.6 1.2 concatenate.9
  29.9 0.4 fusion.94
  30.3 8.1 %while.1 = (s32[]{:T(128)}, bf16[896,576]{1,0:T(8,128)(2,1)S(1)}, s32[4,2]{0,1:T(2,128)S(1)}, bf16[4,384,576]{2,1,0:T(8,128)(2,1)}, s32[]{:T(128)}) while((s32[]{:T(128)}, bf16[896,576]{1,0:T(8,128)(2,1)S(1)}, s32[4,2]{0,1:T(2,128)S(1)}, bf16[4,384,576]{2,1,0:T(8,128)(2,1)}, s32[]{:T(128)}) %tuple.22), condition=%wide.while_cond, body=%wide.while_body.sunk | while | flops 2 | bytes 935001 | solution.py:63
  30.4 0.5 slice.58
  30.9 1.5 bitcast_dynamic-update-slice_fusion.2
  32.4 0.5 slice.58
  32.9 1.5 bitcast_dynamic-update-slice_fusion.2
  34.4 0.5 slice.58
  34.9 1.4 bitcast_dynamic-update-slice_fusion.2
  36.4 0.5 slice.58
  36.9 1.5 bitcast_dynamic-update-slice_fusion.2
  38.4 3.0 fusion.93
  41.3 14.2 %all-to-all-done = bf16[32,2,16,576]{3,2,1,0:T(8,128)(2,1)} async-done(((bf16[32,2,16,576]{3,2,1,0:T(8,128)(2,1)}), bf16[32,2,16,576]{3,2,1,0:T(8,128)(2,1)}, u32[]{:S(2)}, u32[]{:S(2)}) %all-to-all-start) | async-done | bytes 1179680 | tf_op jit(solution)/shard_map/all_to_all | solution.py:97
  55.6 6.0 %fusion.2 = f32[64,2,16,16]{2,3,1,0:T(8,128)S(1)} fusion(bf16[64,16,576,1]{2,1,3,0:T(8,128)(2,1)} %bitcast.13, bf16[64,2,16,576]{3,2,1,0:T(8,128)(2,1)} %gather_fusion, pred[64]{0:T(512)(128)(4,1)S(1)} %compare_and_fusion.3), kind=kOutput, calls=%fused_computation.14 | convolution fusion | flops 38928384 | bytes 3670080 | tf_op jit(solution)/shard_map/nthc,nbc->nthb/dot_general | solution.py:108
  61.5 0.7 copy.176
  62.4 0.7 gather_fusion.1
  63.1 1.1 fusion.51
  64.7 0.9 copy.180
  65.5 1.9 fusion.43
  67.5 3.8 %fusion = f32[4,2,16,512]{3,0,2,1:T(4,128)S(1)} fusion(f32[64,2,16,512]{3,2,1,0:T(8,128)S(1)} %fusion.43, pred[4,64]{1,0:T(4,128)(4,1)S(1)} %fusion.81), kind=kOutput, calls=%fused_computation.12 | convolution fusion | flops 50331648 | bytes 4456704 | tf_op jit(solution)/shard_map/rn,nthc->rthc/dot_general | solution.py:147
  71.5 0.4 fusion.23
  72.0 0.4 fusion.38
  72.5 0.6 copy.236
  73.7 0.8 select_reduce_fusion
  74.6 0.6 gather_fusion.6
  75.4 0.8 fusion.47
  76.2 0.6 gather_fusion.5
  76.9 67.3 %all-gather.2.cloned.1.call-done = bf16[256,2048]{1,0:T(8,128)(2,1)} async-done(((bf16[8,2048]{1,0:T(8,128)(2,1)}), bf16[256,2048]{1,0:T(8,128)(2,1)}) %all-gather.2.cloned.1.call-update) | async-done | bytes 1048592 | tf_op jit(solution)/shard_map/all_gather | solution.py:156
  144.2 2.4 convolution_convert_fusion.2
  146.6 64.4 %all-reduce.4.cloned.1.call-done = bf16[256,224]{0,1:T(8,128)(2,1)} async-done(((bf16[256,224]{0,1:T(8,128)(2,1)}), bf16[256,224]{0,1:T(8,128)(2,1)}) %all-reduce.4.cloned.1.call-update) | async-done | bytes 114704 | tf_op jit(solution)/shard_map/psum | solution.py:158
  211.0 0.9 add_convert_fusion
  212.1 4.1 %gather_fusion.7 = bf16[1280,224]{1,0:T(8,128)(2,1)S(1)} fusion(bf16[128,224]{1,0:T(8,128)(2,1)S(1)} %copy.194, s32[2048]{0:T(1024)S(1)} %pad_clamp_fusion), kind=kCustom, calls=%fused_computation.7 | custom fusion | bytes 1152000 | tf_op jit(solution)/shard_map/jit(_take)/gather | solution.py:169
  216.2 1.2 select_select_fusion
  217.4 9.3 %all-to-all-start.1 = ((bf16[32,40,1,224]{3,1,2,0:T(8,128)(2,1)}), bf16[32,40,1,224]{3,1,2,0:T(8,128)(2,1)S(1)}, u32[]{:S(2)}, u32[]{:S(2)}) async-start(bf16[32,40,1,224]{3,1,2,0:T(8,128)(2,1)} %select_select_fusion), calls=%async_computation.1 | async-start | bytes 1310720 | tf_op jit(solution)/shard_map/all_to_all | solution.py:172
  226.8 17.8 %all-to-all-done.1 = bf16[32,40,1,224]{3,1,2,0:T(8,128)(2,1)S(1)} async-done(((bf16[32,40,1,224]{3,1,2,0:T(8,128)(2,1)}), bf16[32,40,1,224]{3,1,2,0:T(8,128)(2,1)S(1)}, u32[]{:S(2)}, u32[]{:S(2)}) %all-to-all-start.1) | async-done | bytes 573472 | tf_op jit(solution)/shard_map/all_to_all | solution.py:172
  244.7 0.8 copy-done.1
  245.4 1.5 copy.196
  246.9 2.1 reshape.672
  249.0 1.4 fusion.12
  250.4 2.9 fusion.91
  253.3 6.1 %convolution_convert_fusion = bf16[40,7168]{1,0:T(8,128)(2,1)} fusion(bf16[256,7168]{1,0:T(8,128)(2,1)} %param.29, bf16[7168,256]{1,0:T(8,128)(2,1)} %param.28, f32[40,256]{1,0:T(8,128)S(1)} %fusion.91, f32[40,7168]{1,0:T(8,128)S(1)} %reshape.672, f32[7168]{0:T(1024)S(1)} %copy-done.8, f32[40]{0:T(128)S(1)} %add_rsqrt_fusion), kind=kOutput, calls=%fused_computation.11 | convolution fusion | flops 294809600 | bytes 9130144 | tf_op jit(solution)/shard_map/dot_general | solution.py:182
  259.4 3.7 %convert_element_type.126 = bf16[1,40,128,56]{3,2,1,0:T(8,128)(2,1)S(1)} reshape(bf16[40,7168]{1,0:T(8,128)(2,1)} %convolution_convert_fusion) | data formatting | bytes 1146880 | tf_op jit(solution)/shard_map/convert_element_type | solution.py:184
  263.1 1.9 copy.237
  265.0 3.7 %reshape.761 = bf16[128,2,1120]{2,1,0:T(2,128)(2,1)} reshape(bf16[128,1,40,56]{3,2,1,0:T(8,128)(2,1)} %bitcast.155) | data formatting | bytes 1146880
  268.8 11.8 %all-to-all-start.2 = ((bf16[128,2,1120]{2,1,0:T(2,128)(2,1)}), bf16[128,2,1120]{2,1,0:T(2,128)(2,1)}, u32[]{:S(2)}, u32[]{:S(2)}) async-start(bf16[128,2,1120]{2,1,0:T(2,128)(2,1)} %reshape.761), calls=%async_computation.2 | async-start | bytes 1179648 | tf_op jit(solution)/shard_map/all_to_all | solution.py:183
  280.5 0.6 gather_fusion.2
  281.2 0.7 gather_fusion.3
  282.1 33.0 %gather_fusion.4 = f32[5120]{0:T(1024)S(1)} fusion(f32[128,16]{0,1:T(8,128)S(1)} %select_reduce_fusion.2, s32[5120]{0:T(1024)S(1)} %reshape.708), kind=kCustom, calls=%fused_computation.4 | custom fusion | bytes 81920 | tf_op jit(solution)/shard_map/gather | solution.py:205
  315.5 0.7 broadcast_select_fusion.1
  316.2 0.7 reshape.740
  317.1 3.4 reshape.762
  320.5 1.7 bitcast_convert_fusion
  322.1 2.1 copy.217
  324.3 1.1 broadcast_multiply_fusion
  325.4 3.0 copy.200
  328.4 28.2 %scatter_fusion = f32[128,56]{1,0:T(8,128)S(1)} fusion(f32[128,56]{1,0:T(8,128)S(1)} %copy.199, s32[5120]{0:T(1024)S(1)} %copy-done.9, f32[5120,56]{1,0:T(8,128)} %copy.200), kind=kCustom, calls=%fused_computation.8 | custom fusion | flops 286720 | bytes 3461120 | tf_op jit(solution)/shard_map/scatter-add | solution.py:209
  356.6 0.7 copy.201
  (109 shorter events, 4.8 us)
Async XLA Ops:
  6.5 65.4 %copy-start = (bf16[16,512,128]{2,1,0:T(8,128)(2,1)S(1)}, bf16[16,512,128]{2,1,0:T(8,128)(2,1)}, u32[]{:S(2)}) copy-start(bf16[16,512,128]{2,1,0:T(8,128)(2,1)} %param.21) | copy-start | bytes 6291460
  11.4 13.0 %copy-start.14 = (s32[1,4]{1,0:T(1,128)S(1)}, s32[1,4]{1,0:T(1,128)}, u32[]{:S(2)}) copy-start(s32[1,4]{1,0:T(1,128)} %param.18) | copy-start | bytes 52
  11.4 13.3 %copy-start.10 = (bf16[8,576]{1,0:T(8,128)(2,1)S(1)}, bf16[8,576]{1,0:T(8,128)(2,1)}, u32[]{:S(2)}) copy-start(bf16[8,576]{1,0:T(8,128)(2,1)} %param.16) | copy-start | bytes 27652
  11.4 13.4 %copy-start.6 = (bf16[8,9216]{1,0:T(8,128)(2,1)S(1)}, bf16[8,9216]{1,0:T(8,128)(2,1)}, u32[]{:S(2)}) copy-start(bf16[8,9216]{1,0:T(8,128)(2,1)} %param.15) | copy-start | bytes 442372
  11.4 13.8 %copy-start.5 = (bf16[512,576]{0,1:T(8,128)(2,1)S(1)}, bf16[512,576]{0,1:T(8,128)(2,1)}, u32[]{:S(2)}) copy-start(bf16[512,576]{0,1:T(8,128)(2,1)} %param.17) | copy-start | bytes 1769476
  11.4 44.1 %all-to-all-start = ((bf16[32,2,16,576]{3,2,1,0:T(8,128)(2,1)}), bf16[32,2,16,576]{3,2,1,0:T(8,128)(2,1)}, u32[]{:S(2)}, u32[]{:S(2)}) async-start(bf16[32,2,16,576]{3,2,1,0:T(8,128)(2,1)} %copy.175), calls=%async_computation | async-start | bytes 2621440 | tf_op jit(solution)/shard_map/all_to_all | solution.py:97
  23.7 120.5 %all-gather.2.cloned.1.call-start = ((), (), s32[]{:S(2)}) async-start(), calls=%async_computation.3 | async-start | bytes 1081344 | tf_op jit(solution)/shard_map/all_gather | solution.py:156
  67.4 4.1 %copy-start.2 = (bf16[4,384,576]{2,1,0:T(8,128)(2,1)S(1)}, bf16[4,384,576]{2,1,0:T(8,128)(2,1)}, u32[]{:S(2)}) copy-start(bf16[4,384,576]{2,1,0:T(8,128)(2,1)} %get-tuple-element.12) | copy-start | bytes 5308420
  67.4 4.1 %copy-start.4 = (f32[4,2,16,384]{3,2,1,0:T(8,128)S(1)}, f32[4,2,16,384]{3,2,1,0:T(8,128)}, u32[]{:S(2)}) copy-start(f32[4,2,16,384]{3,2,1,0:T(8,128)} %get-tuple-element.28) | copy-start | bytes 589828
  72.0 1.4 copy-start.13
  72.0 72.2 %copy-start.3 = (bf16[2048,224]{0,1:T(8,128)(2,1)S(1)}, bf16[2048,224]{0,1:T(8,128)(2,1)}, u32[]{:S(2)}) copy-start(bf16[2048,224]{0,1:T(8,128)(2,1)} %param.22) | copy-start | bytes 2752516
  72.4 138.6 %copy-start.7 = (bf16[256,224]{0,1:T(8,128)(2,1)S(1)}, bf16[256,224]{0,1:T(8,128)(2,1)}, u32[]{:S(2)}) copy-start(bf16[256,224]{0,1:T(8,128)(2,1)} %param.23) | copy-start | bytes 344068
  73.1 137.9 %all-reduce.4.cloned.1.call-start = ((), (), s32[]{:S(2)}) async-start(), calls=%async_computation.4 | async-start | bytes 229376 | tf_op jit(solution)/shard_map/psum | solution.py:158
  217.4 27.2 %all-to-all-start.1 = ((bf16[32,40,1,224]{3,1,2,0:T(8,128)(2,1)}), bf16[32,40,1,224]{3,1,2,0:T(8,128)(2,1)S(1)}, u32[]{:S(2)}, u32[]{:S(2)}) async-start(bf16[32,40,1,224]{3,1,2,0:T(8,128)(2,1)} %select_select_fusion), calls=%async_computation.1 | async-start | bytes 1310720 | tf_op jit(solution)/shard_map/all_to_all | solution.py:172
  226.8 88.5 %copy-start.11 = (pred[128]{0:T(512)(128)(4,1)}, pred[128]{0:T(512)(128)(4,1)S(1)}, u32[]{:S(2)}) copy-start(pred[128]{0:T(512)(128)(4,1)S(1)} %compare_and_fusion.2) | copy-start | bytes 388
  244.6 0.9 copy-start.1
  246.9 3.5 copy-start.8
  265.0 16.8 %copy-start.12 = (f32[256,4]{0,1:T(4,128)S(1)}, f32[256,4]{0,1:T(4,128)}, u32[]{:S(2)}) copy-start(f32[256,4]{0,1:T(4,128)} %param.26) | copy-start | bytes 12292
  268.8 48.3 %all-to-all-start.2 = ((bf16[128,2,1120]{2,1,0:T(2,128)(2,1)}), bf16[128,2,1120]{2,1,0:T(2,128)(2,1)}, u32[]{:S(2)}, u32[]{:S(2)}) async-start(bf16[128,2,1120]{2,1,0:T(2,128)(2,1)} %reshape.761), calls=%async_computation.2 | async-start | bytes 1179648 | tf_op jit(solution)/shard_map/all_to_all | solution.py:183
  325.4 3.0 copy-start.9
Sparse Core Ops, SparseCore 0:
  73.2 70.9 all-gather.1
  146.7 64.2 all-reduce.3
where the time goes:
time: 365 us; the launch traced here: 364 us
  waiting for transfers between devices  164 us (45%)
  local copies, waits for them, and re-layouts  82.7 us (23%)
  other arithmetic  40.5 us (11%)
  starting transfers between devices  33.9 us (9%)
  matrix products  29.1 us (8%)
  between operations  14 us (4%)
    all_gather x1, waiting for transfers between devices, per_device(): lax.all_gather(values, 'attn', axis=0, tiled=True)  67.3 us
    psum x1, waiting for transfers between devices, per_device(): lax.psum(partial_cols.astype(jnp.bfloat16), ('expert', 'rep'))  64.4 us
    gather x2, local copies, waits for them, and re-layouts, per_device(): share_table[back_rows, source_expert[:, None]]  33.1 us
    scatter-add x1, other arithmetic, per_device(): jax.ops.segment_sum(weighted, back_rows.reshape(-1), num_segments=rows_part)  28.2 us
    all_to_all x1, waiting for transfers between devices, per_device(): lax.all_to_all(outgoing_rows, 'attn', split_axis=0, concat_axis=2, tiled=...  17.8 us
    all_to_all x1, waiting for transfers between devices, per_device(): lax.all_to_all(outgoing, 'attn', split_axis=0, concat_axis=0, tiled=True)  14.2 us
    all_to_all x1, starting transfers between devices, per_device(): lax.all_to_all(outgoing, 'attn', split_axis=0, concat_axis=0, tiled=True)  12.3 us
    all_to_all x1, starting transfers between devices, per_device(): lax.all_to_all(result.reshape(1, item_count, n_attn * n_expert, -1).astyp...  11.8 us
  transfers between devices with their start and end apart: 5, of which 4 were waited for; matrix products, arithmetic and copies ran while one was open for 16% of the time, Pallas kernels for 0%

commit v1 on v0

--- a/solution.py
+++ b/solution.py
@@ -153,7 +153,11 @@
     ).astype(jnp.bfloat16)
     values = values.reshape(2 * req_count, head_count * w_uv.shape[2])
     partial_cols = jnp.dot(
-        lax.all_gather(values, "attn", axis=0, tiled=True), w_o, preferred_element_type=jnp.float32
+        jnp.concatenate(
+            lax.all_to_all(jnp.stack([values] * lax.axis_size("attn")), "attn", 0, 0), axis=0
+        ),
+        w_o,
+        preferred_element_type=jnp.float32,
     )
     attn_cols = lax.psum(partial_cols.astype(jnp.bfloat16), ("expert", "rep")).astype(jnp.float32)
     hidden_cols = (residual.astype(jnp.float32) + attn_cols).astype(jnp.bfloat16)

time: 365 us -> 324 us (0.89)
  waiting for transfers between devices: 164 us -> 116 us
  starting transfers between devices: 33.9 us -> 39.6 us
    all_gather x1 -> x0, waiting for transfers between devices: 67.3 us -> none  [per_device(): lax.all_gather(values, 'attn', axis=0, tiled=True)]
    all_to_all x0 -> x1, waiting for transfers between devices: none -> 21.4 us  [per_device(): lax.all_to_all(jnp.stack([values] * lax.axis_size('attn')), 'attn', 0, 0)]
    all_to_all x0 -> x1, starting transfers between devices: none -> 6.29 us  [per_device(): lax.all_to_all(jnp.stack([values] * lax.axis_size('attn')), 'attn', 0, 0)]
    unnamed x34 -> x32, local copies, waits for them, and re-layouts: 9.59 us -> 8.99 us
  transfers between devices with their start and end apart: 5 -> 5, of which waited for: 4 -> 4; matrix products, arithmetic and copies ran while one was open for 16% -> 18% of each run, Pallas kernels for 0% -> 0%
where the time goes in v1:
time: 324 us; the launch traced here: 323 us
  waiting for transfers between devices  116 us (36%)
  local copies, waits for them, and re-layouts  83.2 us (26%)
  other arithmetic  40.5 us (12%)
  starting transfers between devices  39.6 us (12%)
  matrix products  29.1 us (9%)
  between operations  14 us (4%)
    psum x1, waiting for transfers between devices, per_device(): lax.psum(partial_cols.astype(jnp.bfloat16), ('expert', 'rep'))  62.5 us
    gather x2, local copies, waits for them, and re-layouts, per_device(): share_table[back_rows, source_expert[:, None]]  33.1 us
    scatter-add x1, other arithmetic, per_device(): jax.ops.segment_sum(weighted, back_rows.reshape(-1), num_segments=rows_part)  28.2 us
    all_to_all x1, waiting for transfers between devices, per_device(): lax.all_to_all(jnp.stack([values] * lax.axis_size('attn')), 'attn', 0, 0)  21.4 us
    all_to_all x1, waiting for transfers between devices, per_device(): lax.all_to_all(outgoing_rows, 'attn', split_axis=0, concat_axis=2, tiled=...  17.8 us
    all_to_all x1, waiting for transfers between devices, per_device(): lax.all_to_all(outgoing, 'attn', split_axis=0, concat_axis=0, tiled=True)  14.5 us
    all_to_all x1, starting transfers between devices, per_device(): lax.all_to_all(outgoing, 'attn', split_axis=0, concat_axis=0, tiled=True)  12.3 us
    all_to_all x1, starting transfers between devices, per_device(): lax.all_to_all(result.reshape(1, item_count, n_attn * n_expert, -1).astyp...  11.5 us
  transfers between devices with their start and end apart: 5, of which 4 were waited for; matrix products, arithmetic and copies ran while one was open for 18% of the time, Pallas kernels for 0%

profile of v1, /device:TPU:1, one launch (start us, length us, event | category | flops | bytes accessed | tf_op | source)
XLA Modules:
  0.0 322.8 jit_solution(4314252654612775551)
XLA Ops:
  6.5 0.9 reshape.651
  7.5 0.8 convert_reduce_fusion
  8.3 1.6 convolution_convert_fusion.1
  9.9 1.5 copy.175
  11.4 12.3 %all-to-all-start = ((bf16[32,2,16,576]{3,2,1,0:T(8,128)(2,1)}), bf16[32,2,16,576]{3,2,1,0:T(8,128)(2,1)}, u32[]{:S(2)}, u32[]{:S(2)}) async-start(bf16[32,2,16,576]{3,2,1,0:T(8,128)(2,1)} %copy.175), calls=%async_computation | async-start | bytes 2621440 | tf_op jit(solution)/shard_map/all_to_all | solution.py:97
  25.0 1.1 copy.169
  26.0 2.4 gather_fusion
  28.4 1.2 concatenate.9
  30.1 8.1 %while.1 = (s32[]{:T(128)}, bf16[896,576]{1,0:T(8,128)(2,1)S(1)}, s32[4,2]{0,1:T(2,128)S(1)}, bf16[4,384,576]{2,1,0:T(8,128)(2,1)}, s32[]{:T(128)}) while((s32[]{:T(128)}, bf16[896,576]{1,0:T(8,128)(2,1)S(1)}, s32[4,2]{0,1:T(2,128)S(1)}, bf16[4,384,576]{2,1,0:T(8,128)(2,1)}, s32[]{:T(128)}) %tuple.22), condition=%wide.while_cond, body=%wide.while_body.sunk | while | flops 2 | bytes 935001 | solution.py:63
  30.1 0.5 slice.58
  30.6 1.5 bitcast_dynamic-update-slice_fusion.2
  32.2 0.5 slice.58
  32.7 1.5 bitcast_dynamic-update-slice_fusion.2
  34.2 0.5 slice.58
  34.7 1.4 bitcast_dynamic-update-slice_fusion.2
  36.2 0.5 slice.58
  36.7 1.5 bitcast_dynamic-update-slice_fusion.2
  38.1 3.0 fusion.94
  41.1 14.5 %all-to-all-done = bf16[32,2,16,576]{3,2,1,0:T(8,128)(2,1)} async-done(((bf16[32,2,16,576]{3,2,1,0:T(8,128)(2,1)}), bf16[32,2,16,576]{3,2,1,0:T(8,128)(2,1)}, u32[]{:S(2)}, u32[]{:S(2)}) %all-to-all-start) | async-done | bytes 1179680 | tf_op jit(solution)/shard_map/all_to_all | solution.py:97
  55.6 6.0 %fusion.2 = f32[64,2,16,16]{2,3,1,0:T(8,128)S(1)} fusion(bf16[64,16,576,1]{2,1,3,0:T(8,128)(2,1)} %bitcast.13, bf16[64,2,16,576]{3,2,1,0:T(8,128)(2,1)} %gather_fusion, pred[64]{0:T(512)(128)(4,1)S(1)} %compare_and_fusion.3), kind=kOutput, calls=%fused_computation.14 | convolution fusion | flops 38928384 | bytes 3670080 | tf_op jit(solution)/shard_map/nthc,nbc->nthb/dot_general | solution.py:108
  61.5 0.7 copy.176
  62.4 0.7 gather_fusion.1
  63.1 1.1 fusion.52
  64.7 0.9 copy.180
  65.5 1.9 fusion.43
  67.5 3.8 %fusion = f32[4,2,16,512]{3,0,2,1:T(4,128)S(1)} fusion(f32[64,2,16,512]{3,2,1,0:T(8,128)S(1)} %fusion.43, pred[4,64]{1,0:T(4,128)(4,1)S(1)} %fusion.82), kind=kOutput, calls=%fused_computation.12 | convolution fusion | flops 50331648 | bytes 4456704 | tf_op jit(solution)/shard_map/rn,nthc->rthc/dot_general | solution.py:147
  71.5 0.4 fusion.23
  72.0 0.4 fusion.38
  72.4 1.1 stack.3
  73.6 6.3 %all-to-all-start.1 = ((bf16[32,8,2048]{2,1,0:T(8,128)(2,1)}), bf16[32,8,2048]{2,1,0:T(8,128)(2,1)S(1)}, u32[]{:S(2)}, u32[]{:S(2)}) async-start(bf16[32,8,2048]{2,1,0:T(8,128)(2,1)} %stack.3), calls=%async_computation.1 | async-start | bytes 2097152 | tf_op jit(solution)/shard_map/all_to_all | solution.py:157
  80.5 0.8 select_reduce_fusion
  81.4 0.6 gather_fusion.6
  82.1 0.8 fusion.48
  83.0 0.6 gather_fusion.5
  83.7 21.4 %all-to-all-done.1 = bf16[32,8,2048]{2,1,0:T(8,128)(2,1)S(1)} async-done(((bf16[32,8,2048]{2,1,0:T(8,128)(2,1)}), bf16[32,8,2048]{2,1,0:T(8,128)(2,1)S(1)}, u32[]{:S(2)}, u32[]{:S(2)}) %all-to-all-start.1) | async-done | bytes 1048608 | tf_op jit(solution)/shard_map/all_to_all | solution.py:157
  105.1 2.3 convolution_convert_fusion.2
  107.5 62.5 %all-reduce.4.cloned.1.call-done = bf16[256,224]{0,1:T(8,128)(2,1)} async-done(((bf16[256,224]{0,1:T(8,128)(2,1)}), bf16[256,224]{0,1:T(8,128)(2,1)}) %all-reduce.4.cloned.1.call-update) | async-done | bytes 114704 | tf_op jit(solution)/shard_map/psum | solution.py:162
  170.0 0.9 add_convert_fusion
  171.0 4.1 %gather_fusion.7 = bf16[1280,224]{1,0:T(8,128)(2,1)S(1)} fusion(bf16[128,224]{1,0:T(8,128)(2,1)S(1)} %copy.194, s32[2048]{0:T(1024)S(1)} %pad_clamp_fusion), kind=kCustom, calls=%fused_computation.7 | custom fusion | bytes 1152000 | tf_op jit(solution)/shard_map/jit(_take)/gather | solution.py:173
  175.1 1.2 select_select_fusion
  176.3 9.3 %all-to-all-start.2 = ((bf16[32,40,1,224]{3,1,2,0:T(8,128)(2,1)}), bf16[32,40,1,224]{3,1,2,0:T(8,128)(2,1)S(1)}, u32[]{:S(2)}, u32[]{:S(2)}) async-start(bf16[32,40,1,224]{3,1,2,0:T(8,128)(2,1)} %select_select_fusion), calls=%async_computation.2 | async-start | bytes 1310720 | tf_op jit(solution)/shard_map/all_to_all | solution.py:176
  185.7 17.8 %all-to-all-done.2 = bf16[32,40,1,224]{3,1,2,0:T(8,128)(2,1)S(1)} async-done(((bf16[32,40,1,224]{3,1,2,0:T(8,128)(2,1)}), bf16[32,40,1,224]{3,1,2,0:T(8,128)(2,1)S(1)}, u32[]{:S(2)}, u32[]{:S(2)}) %all-to-all-start.2) | async-done | bytes 573472 | tf_op jit(solution)/shard_map/all_to_all | solution.py:176
  203.6 0.8 copy-done.1
  204.4 1.5 copy.196
  205.8 2.1 reshape.674
  207.9 1.4 fusion.12
  209.3 2.9 fusion.92
  212.2 6.1 %convolution_convert_fusion = bf16[40,7168]{1,0:T(8,128)(2,1)} fusion(bf16[256,7168]{1,0:T(8,128)(2,1)} %param.29, bf16[7168,256]{1,0:T(8,128)(2,1)} %param.28, f32[40,256]{1,0:T(8,128)S(1)} %fusion.92, f32[40,7168]{1,0:T(8,128)S(1)} %reshape.674, f32[7168]{0:T(1024)S(1)} %copy-done.7, f32[40]{0:T(128)S(1)} %add_rsqrt_fusion), kind=kOutput, calls=%fused_computation.11 | convolution fusion | flops 294809600 | bytes 9130144 | tf_op jit(solution)/shard_map/dot_general | solution.py:186
  218.3 3.7 %convert_element_type.126 = bf16[1,40,128,56]{3,2,1,0:T(8,128)(2,1)S(1)} reshape(bf16[40,7168]{1,0:T(8,128)(2,1)} %convolution_convert_fusion) | data formatting | bytes 1146880 | tf_op jit(solution)/shard_map/convert_element_type | solution.py:188
  222.0 1.9 copy.237
  223.9 3.7 %reshape.763 = bf16[128,2,1120]{2,1,0:T(2,128)(2,1)} reshape(bf16[128,1,40,56]{3,2,1,0:T(8,128)(2,1)} %bitcast.157) | data formatting | bytes 1146880
  227.7 11.5 %all-to-all-start.3 = ((bf16[128,2,1120]{2,1,0:T(2,128)(2,1)}), bf16[128,2,1120]{2,1,0:T(2,128)(2,1)}, u32[]{:S(2)}, u32[]{:S(2)}) async-start(bf16[128,2,1120]{2,1,0:T(2,128)(2,1)} %reshape.763), calls=%async_computation.3 | async-start | bytes 1179648 | tf_op jit(solution)/shard_map/all_to_all | solution.py:187
  239.2 0.6 gather_fusion.2
  239.8 0.7 gather_fusion.3
  240.8 33.0 %gather_fusion.4 = f32[5120]{0:T(1024)S(1)} fusion(f32[128,16]{0,1:T(8,128)S(1)} %select_reduce_fusion.2, s32[5120]{0:T(1024)S(1)} %reshape.710), kind=kCustom, calls=%fused_computation.4 | custom fusion | bytes 81920 | tf_op jit(solution)/shard_map/gather | solution.py:209
  274.1 0.7 broadcast_select_fusion.1
  274.9 0.7 reshape.742
  275.8 3.4 %reshape.764 = bf16[128,1,40,56]{3,2,1,0:T(8,128)(2,1)S(1)} reshape(bf16[128,2,1120]{2,1,0:T(2,128)(2,1)} %all-to-all-done.3) | data formatting | bytes 1146880
  279.1 1.7 bitcast_convert_fusion
  280.8 2.1 copy.217
  282.9 1.1 broadcast_multiply_fusion
  284.0 3.0 copy.200
  287.0 28.2 %scatter_fusion = f32[128,56]{1,0:T(8,128)S(1)} fusion(f32[128,56]{1,0:T(8,128)S(1)} %copy.199, s32[5120]{0:T(1024)S(1)} %copy-done.8, f32[5120,56]{1,0:T(8,128)} %copy.200), kind=kCustom, calls=%fused_computation.8 | custom fusion | flops 286720 | bytes 3461120 | tf_op jit(solution)/shard_map/scatter-add | solution.py:213
  315.2 0.7 copy.201
  (107 shorter events, 4.9 us)
Async XLA Ops:
  6.5 65.4 %copy-start = (bf16[16,512,128]{2,1,0:T(8,128)(2,1)S(1)}, bf16[16,512,128]{2,1,0:T(8,128)(2,1)}, u32[]{:S(2)}) copy-start(bf16[16,512,128]{2,1,0:T(8,128)(2,1)} %param.21) | copy-start | bytes 6291460
  11.4 12.8 %copy-start.13 = (s32[1,4]{1,0:T(1,128)S(1)}, s32[1,4]{1,0:T(1,128)}, u32[]{:S(2)}) copy-start(s32[1,4]{1,0:T(1,128)} %param.18) | copy-start | bytes 52
  11.4 13.1 %copy-start.9 = (bf16[8,576]{1,0:T(8,128)(2,1)S(1)}, bf16[8,576]{1,0:T(8,128)(2,1)}, u32[]{:S(2)}) copy-start(bf16[8,576]{1,0:T(8,128)(2,1)} %param.16) | copy-start | bytes 27652
  11.4 13.1 %copy-start.5 = (bf16[8,9216]{1,0:T(8,128)(2,1)S(1)}, bf16[8,9216]{1,0:T(8,128)(2,1)}, u32[]{:S(2)}) copy-start(bf16[8,9216]{1,0:T(8,128)(2,1)} %param.15) | copy-start | bytes 442372
  11.4 13.5 %copy-start.4 = (bf16[512,576]{0,1:T(8,128)(2,1)S(1)}, bf16[512,576]{0,1:T(8,128)(2,1)}, u32[]{:S(2)}) copy-start(bf16[512,576]{0,1:T(8,128)(2,1)} %param.17) | copy-start | bytes 1769476
  11.4 44.1 %all-to-all-start = ((bf16[32,2,16,576]{3,2,1,0:T(8,128)(2,1)}), bf16[32,2,16,576]{3,2,1,0:T(8,128)(2,1)}, u32[]{:S(2)}, u32[]{:S(2)}) async-start(bf16[32,2,16,576]{3,2,1,0:T(8,128)(2,1)} %copy.175), calls=%async_computation | async-start | bytes 2621440 | tf_op jit(solution)/shard_map/all_to_all | solution.py:97
  67.4 4.1 %copy-start.2 = (bf16[4,384,576]{2,1,0:T(8,128)(2,1)S(1)}, bf16[4,384,576]{2,1,0:T(8,128)(2,1)}, u32[]{:S(2)}) copy-start(bf16[4,384,576]{2,1,0:T(8,128)(2,1)} %get-tuple-element.12) | copy-start | bytes 5308420
  67.4 4.1 %copy-start.3 = (f32[4,2,16,384]{3,2,1,0:T(8,128)S(1)}, f32[4,2,16,384]{3,2,1,0:T(8,128)}, u32[]{:S(2)}) copy-start(f32[4,2,16,384]{3,2,1,0:T(8,128)} %get-tuple-element.28) | copy-start | bytes 589828
  72.4 7.7 %copy-start.12 = (s32[256,4]{0,1:T(4,128)S(1)}, s32[256,4]{0,1:T(4,128)}, u32[]{:S(2)}) copy-start(s32[256,4]{0,1:T(4,128)} %param.25) | copy-start | bytes 12292
  73.6 31.5 %all-to-all-start.1 = ((bf16[32,8,2048]{2,1,0:T(8,128)(2,1)}), bf16[32,8,2048]{2,1,0:T(8,128)(2,1)S(1)}, u32[]{:S(2)}, u32[]{:S(2)}) async-start(bf16[32,8,2048]{2,1,0:T(8,128)(2,1)} %stack.3), calls=%async_computation.1 | async-start | bytes 2097152 | tf_op jit(solution)/shard_map/all_to_all | solution.py:157
  79.9 90.1 %copy-start.6 = (bf16[256,224]{0,1:T(8,128)(2,1)S(1)}, bf16[256,224]{0,1:T(8,128)(2,1)}, u32[]{:S(2)}) copy-start(bf16[256,224]{0,1:T(8,128)(2,1)} %param.23) | copy-start | bytes 344068
  79.9 90.1 %all-reduce.4.cloned.1.call-start = ((), (), s32[]{:S(2)}) async-start(), calls=%async_computation.4 | async-start | bytes 229376 | tf_op jit(solution)/shard_map/psum | solution.py:162
  176.3 27.2 %all-to-all-start.2 = ((bf16[32,40,1,224]{3,1,2,0:T(8,128)(2,1)}), bf16[32,40,1,224]{3,1,2,0:T(8,128)(2,1)S(1)}, u32[]{:S(2)}, u32[]{:S(2)}) async-start(bf16[32,40,1,224]{3,1,2,0:T(8,128)(2,1)} %select_select_fusion), calls=%async_computation.2 | async-start | bytes 1310720 | tf_op jit(solution)/shard_map/all_to_all | solution.py:176
  185.7 88.2 %copy-start.10 = (pred[128]{0:T(512)(128)(4,1)}, pred[128]{0:T(512)(128)(4,1)S(1)}, u32[]{:S(2)}) copy-start(pred[128]{0:T(512)(128)(4,1)S(1)} %compare_and_fusion.2) | copy-start | bytes 388
  203.5 0.9 copy-start.1
  205.8 3.5 %copy-start.7 = (f32[7168]{0:T(1024)S(1)}, f32[7168]{0:T(1024)}, u32[]{:S(2)}) copy-start(f32[7168]{0:T(1024)} %param.24) | copy-start | bytes 86020
  223.9 16.6 %copy-start.11 = (f32[256,4]{0,1:T(4,128)S(1)}, f32[256,4]{0,1:T(4,128)}, u32[]{:S(2)}) copy-start(f32[256,4]{0,1:T(4,128)} %param.26) | copy-start | bytes 12292
  227.7 48.1 %all-to-all-start.3 = ((bf16[128,2,1120]{2,1,0:T(2,128)(2,1)}), bf16[128,2,1120]{2,1,0:T(2,128)(2,1)}, u32[]{:S(2)}, u32[]{:S(2)}) async-start(bf16[128,2,1120]{2,1,0:T(2,128)(2,1)} %reshape.763), calls=%async_computation.3 | async-start | bytes 1179648 | tf_op jit(solution)/shard_map/all_to_all | solution.py:187
  284.0 3.0 copy-start.8
Sparse Core Ops, SparseCore 0:
  107.6 62.3 all-reduce.3
